TPU v7x, 128 devices: a whole 4x4x4 slice. The times are simulated.
128 devices in a mesh: seq: 16 (over y, x), expert: 4 (over z), mp: 2 (over core).
Axes of the slice: x: 4, y: 4, z: 4, core: 2. Of those that a mesh axis runs over, the one named last changes fastest.
Arguments:
- activations: bfloat16 [16384, 4096], P('seq', ('expert', 'mp')), may hold values from -6 to 6
- output_gradient: bfloat16 [16384, 4096], P('seq', ('expert', 'mp')), may hold values from -1.5 to 1.5
- input_state_map: bfloat16 [16384, 16], P('seq'), may hold values from -3 to 3
- output_state_map: bfloat16 [16384, 16], P('seq'), may hold values from -3 to 3
- head_decay_speed: float32 [64], P(('expert', 'mp')), may hold values from 3.0517578e-06 to 0.05, as said below
- spike_decay_level: int32 [16384], P('seq'), may hold values from 0 to 2, as said below
- assign: int32 [128], replicated, may hold values from 0 to 15, as said below
- expert_up_weight: bfloat16 [4, 4096, 12288], P('expert', 'mp', 'seq'), may hold values from -0.09375 to 0.09375
- expert_down_weight: bfloat16 [4, 12288, 4096], P('expert', 'seq', 'mp'), may hold values from -0.0546875 to 0.0546875
Outputs:
- grad_x: float32 [16384, 4096], P('seq', ('expert', 'mp'))
- grad_w_up: float32 [4, 4096, 12288], P('expert', 'mp', 'seq')
- grad_w_down: float32 [4, 12288, 4096], P('expert', 'seq', 'mp')
Inputs may be any that keep to these rules, and one draw needn't show every extreme that they name: `head_decay_speed`: some of the heads keep a tenth or more of their state over the whole sequence, the others lose it within some tens of tokens. `spike_decay_level`: at most three tokens of the sequence have a nonzero level. `assign`: numbers below 4 are the window's experts: the 8 blocks of one index of seq hold at most one block of each of them, each takes at most 8 blocks in all, and one takes exactly 8.
All inputs are finite; a program needn't handle non-finite values.
Results may differ from a plain program's by a relative error of at most 0.019.
Values may be sent and summed in bfloat16 or wider, within the bound.
No kernel may reach another device: no remote copies, remote signals or barrier semaphores. Data moves between devices by JAX's collectives and lax.ppermute only.
A program may use at most 128 MiB of HBM per device.

v0:
```python
import jax
import jax.numpy as jnp
from jax import lax
from jax.sharding import PartitionSpec as P

HEAD = 64
STATE = 16
BLOCK = 128
spike_position_step = 0.3
highest = lax.Precision.HIGHEST


def from_behind(value, axis, steps):
    count = lax.axis_size(axis)
    first, last = (max(0, -steps), min(count, count - steps))
    return lax.ppermute(value, axis, [(source, source + steps) for source in range(first, last)])


def rounded(rounded_in):
    return lax.optimization_barrier(rounded_in.astype(jnp.bfloat16)).astype(jnp.float32)


def split_parts(values):
    high_part = values.astype(jnp.bfloat16)
    low_part = (values - high_part.astype(jnp.float32)).astype(jnp.bfloat16)
    return (high_part, low_part)


def mixing(cum_block, scores, causal):
    spread = cum_block.T[:, :, None] - cum_block.T[:, None, :]
    spread = jnp.where(causal[None], spread, -jnp.inf)
    return jnp.exp(spread) * scores[None]


def narrow(gathered, exp_index, mp_index, half_width):
    row_set = lax.dynamic_index_in_dim(gathered, exp_index, 0, keepdims=False)
    return lax.dynamic_slice_in_dim(row_set, mp_index * half_width, half_width, 1)


def compact(select, gathered, half_width):
    shaped = gathered.reshape(select.shape[1], -1, half_width)
    rows_out = jnp.einsum("js,srf->jrf", select, shaped, preferred_element_type=jnp.float32)
    return rows_out.astype(jnp.bfloat16).reshape(-1, half_width)


def per_device(
    activations,
    output_gradient,
    input_state_map,
    output_state_map,
    head_decay_speed,
    spike_decay_level,
    assign,
    expert_up_weight,
    expert_down_weight,
):
    tokens, slice_width = activations.shape
    heads_dev = slice_width // HEAD
    seq_count = lax.axis_size("seq")
    exp_count = lax.axis_size("expert")
    mp_count = lax.axis_size("mp")
    seq_index = lax.axis_index("seq")
    exp_index = lax.axis_index("expert")
    mp_index = lax.axis_index("mp")
    my_slice = exp_index * mp_count + mp_index
    slice_half = my_slice // exp_count
    half_width = slice_width * exp_count
    slot_total = seq_count // 2
    input_scale = jnp.sqrt(1.0 - jnp.exp(-2.0 * head_decay_speed))
    cum_level = jnp.cumsum(
        -head_decay_speed[None, :]
        - spike_position_step * spike_decay_level.astype(jnp.float32)[:, None],
        axis=0,
    )
    b_float = input_state_map.astype(jnp.float32)
    c_float = output_state_map.astype(jnp.float32)
    act_heads = activations.reshape(tokens, heads_dev, HEAD)
    scaled = act_heads.astype(jnp.float32) * input_scale[None, :, None]
    span_rows = min(512, tokens)
    span_count = tokens // span_rows
    causal = jnp.arange(span_rows)[:, None] >= jnp.arange(span_rows)[None, :]
    zero_level = jnp.zeros((heads_dev,), jnp.float32)
    carry_state = jnp.zeros((heads_dev, HEAD, STATE), jnp.float32)
    pieces = []
    for position in range(span_count):
        first_row = position * span_rows
        last_row = first_row + span_rows
        cum_block = cum_level[first_row:last_row]
        start_level = cum_level[first_row - 1] if position > 0 else zero_level
        scores = jnp.dot(
            output_state_map[first_row:last_row],
            input_state_map[first_row:last_row].T,
            preferred_element_type=jnp.float32,
        )
        weights = mixing(cum_block, scores, causal)
        weight_high, weight_low = split_parts(weights)
        x_span = act_heads[first_row:last_row]
        inner_part = jnp.einsum(
            "hts,shp->thp", weight_high, x_span, preferred_element_type=jnp.float32
        )
        inner_part = inner_part + jnp.einsum(
            "hts,shp->thp", weight_low, x_span, preferred_element_type=jnp.float32
        )
        inner_part = inner_part * input_scale[None, :, None]
        carried = jnp.exp(cum_block - start_level[None, :])[:, :, None] * jnp.einsum(
            "tn,hpn->thp", c_float[first_row:last_row], carry_state, precision=highest
        )
        pieces.append(inner_part + carried)
        end_level = cum_block[-1]
        tail_decay = jnp.exp(end_level[None, :] - cum_block)
        carry_state = jnp.exp(end_level - start_level)[:, None, None] * carry_state + jnp.einsum(
            "shp,sn->hpn",
            scaled[first_row:last_row] * tail_decay[:, :, None],
            b_float[first_row:last_row],
            precision=highest,
        )
    device_decay = jnp.exp(cum_level[-1])
    flat_state = carry_state.reshape(heads_dev, HEAD * STATE)

    def relay_state(rounds, carried_in):
        return from_behind(
            (device_decay[:, None] * carried_in + flat_state).astype(jnp.bfloat16), "seq", 1
        ).astype(jnp.float32)

    incoming = lax.fori_loop(0, seq_count - 1, relay_state, jnp.zeros_like(flat_state))
    incoming = incoming.reshape(heads_dev, HEAD, STATE)
    outputs = jnp.concatenate(pieces, axis=0) + jnp.exp(cum_level)[:, :, None] * jnp.einsum(
        "tn,hpn->thp", c_float, incoming, precision=highest
    )
    mixed_out = (activations.astype(jnp.float32) + outputs.reshape(tokens, slice_width)).astype(
        jnp.bfloat16
    )
    blocks_dev = tokens // BLOCK
    route_table = assign.reshape(seq_count, blocks_dev)
    own_row = lax.dynamic_index_in_dim(route_table, seq_index, 0, keepdims=False)
    chosen = (own_row[None, :] == jnp.arange(exp_count)[:, None]).astype(jnp.bfloat16)
    h_pick = jnp.einsum(
        "eb,brf->erf",
        chosen,
        mixed_out.reshape(blocks_dev, BLOCK, slice_width),
        preferred_element_type=jnp.float32,
    ).astype(jnp.bfloat16)
    g_pick = jnp.einsum(
        "eb,brf->erf",
        chosen,
        output_gradient.reshape(blocks_dev, BLOCK, slice_width),
        preferred_element_type=jnp.float32,
    ).astype(jnp.bfloat16)
    h_full, g_full = (
        lax.all_gather(h_pick, ("expert", "mp"), axis=2, tiled=True),
        lax.all_gather(g_pick, ("expert", "mp"), axis=2, tiled=True),
    )
    h_block = narrow(h_full, exp_index, mp_index, half_width)
    g_block = narrow(g_full, exp_index, mp_index, half_width)
    h_all, g_all = (
        lax.all_gather(h_block, "seq", axis=0, tiled=True),
        lax.all_gather(g_block, "seq", axis=0, tiled=True),
    )
    present = jnp.any(route_table == exp_index, axis=1)
    slot_of = jnp.cumsum(present.astype(jnp.int32)) - 1
    select = ((slot_of[None, :] == jnp.arange(slot_total)[:, None]) & present[None, :]).astype(
        jnp.bfloat16
    )
    x_rows = compact(select, h_all, half_width)
    g_rows = compact(select, g_all, half_width)
    up_local = expert_up_weight[0]
    down_local = expert_down_weight[0]
    pre_act = lax.psum(
        rounded(jnp.dot(x_rows, up_local, preferred_element_type=jnp.float32)).astype(jnp.bfloat16),
        "mp",
    ).astype(jnp.float32)
    activation = jax.nn.silu(pre_act).astype(jnp.bfloat16)
    down_grad = jnp.einsum("tf,td->fd", activation, g_rows, preferred_element_type=jnp.float32)
    act_grad = lax.psum(
        rounded(
            jnp.einsum("td,fd->tf", g_rows, down_local, preferred_element_type=jnp.float32)
        ).astype(jnp.bfloat16),
        "mp",
    ).astype(jnp.float32)
    sigmoid_pre = jax.nn.sigmoid(pre_act)
    pre_grad = (act_grad * sigmoid_pre * (1.0 + pre_act * (1.0 - sigmoid_pre))).astype(jnp.bfloat16)
    up_grad = jnp.einsum("td,tf->df", x_rows, pre_grad, preferred_element_type=jnp.float32)
    row_grad = jnp.einsum("tf,df->td", pre_grad, up_local, preferred_element_type=jnp.float32)
    row_grad = row_grad.astype(jnp.bfloat16).reshape(slot_total, BLOCK, half_width)
    spread_rows = jnp.einsum("js,jrf->srf", select, row_grad, preferred_element_type=jnp.float32)
    back_rows = lax.psum_scatter(
        spread_rows.reshape(BLOCK * lax.axis_size("seq"), half_width).astype(jnp.bfloat16),
        "seq",
        scatter_dimension=0,
        tiled=True,
    )
    arrived = lax.all_gather(back_rows[None], ("expert", "mp"), axis=0, tiled=True)
    halves = lax.dynamic_index_in_dim(
        arrived.reshape(exp_count, mp_count, BLOCK, half_width), slice_half, 1, keepdims=False
    )
    returned = lax.dynamic_slice_in_dim(halves, my_slice % exp_count * slice_width, slice_width, 2)
    token_grad = jnp.einsum("eb,erf->brf", chosen, returned, preferred_element_type=jnp.float32)
    total_grad = output_gradient.astype(jnp.float32) + token_grad.reshape(tokens, slice_width)
    grad_view = total_grad.reshape(tokens, heads_dev, HEAD)
    adjoint = jnp.zeros((heads_dev, HEAD, STATE), jnp.float32)
    back_pieces = [None] * span_count
    for position in reversed(range(span_count)):
        first_row = position * span_rows
        last_row = first_row + span_rows
        cum_block = cum_level[first_row:last_row]
        start_level = cum_level[first_row - 1] if position > 0 else zero_level
        scores = jnp.dot(
            output_state_map[first_row:last_row],
            input_state_map[first_row:last_row].T,
            preferred_element_type=jnp.float32,
        )
        weights = mixing(cum_block, scores, causal)
        weight_high, weight_low = split_parts(weights)
        grad_high, grad_low = split_parts(grad_view[first_row:last_row])
        inner_part = jnp.einsum(
            "hts,thp->shp", weight_high, grad_high, preferred_element_type=jnp.float32
        )
        inner_part = inner_part + jnp.einsum(
            "hts,thp->shp", weight_high, grad_low, preferred_element_type=jnp.float32
        )
        inner_part = inner_part + jnp.einsum(
            "hts,thp->shp", weight_low, grad_high, preferred_element_type=jnp.float32
        )
        end_level = cum_block[-1]
        tail_decay = jnp.exp(end_level[None, :] - cum_block)
        carried = tail_decay[:, :, None] * jnp.einsum(
            "sn,hpn->shp", b_float[first_row:last_row], adjoint, precision=highest
        )
        back_pieces[position] = inner_part + carried
        lead_decay = jnp.exp(cum_block - start_level[None, :])
        adjoint = jnp.exp(end_level - start_level)[:, None, None] * adjoint + jnp.einsum(
            "rhp,rn->hpn",
            grad_view[first_row:last_row] * lead_decay[:, :, None],
            c_float[first_row:last_row],
            precision=highest,
        )
    flat_adjoint = adjoint.reshape(heads_dev, HEAD * STATE)

    def relay_adjoint(rounds, carried_in):
        return from_behind(
            (device_decay[:, None] * carried_in + flat_adjoint).astype(jnp.bfloat16), "seq", -1
        ).astype(jnp.float32)

    later_adjoint = lax.fori_loop(0, seq_count - 1, relay_adjoint, jnp.zeros_like(flat_adjoint))
    later_adjoint = later_adjoint.reshape(heads_dev, HEAD, STATE)
    scan_grad = jnp.concatenate(back_pieces, axis=0) + jnp.exp(cum_level[-1][None, :] - cum_level)[
        :, :, None
    ] * jnp.einsum("sn,hpn->shp", b_float, later_adjoint, precision=highest)
    grad_x = total_grad + (input_scale[None, :, None] * scan_grad).reshape(tokens, slice_width)
    return (grad_x, up_grad[None], down_grad[None])


def solution(mesh):
    in_specs = (
        P("seq", ("expert", "mp")),
        P("seq", ("expert", "mp")),
        P("seq", None),
        P("seq", None),
        P(("expert", "mp")),
        P("seq"),
        P(),
        P("expert", "mp", "seq"),
        P("expert", "seq", "mp"),
    )
    out_specs = (P("seq", ("expert", "mp")), P("expert", "mp", "seq"), P("expert", "seq", "mp"))
    return jax.shard_map(
        per_device, mesh=mesh, in_specs=in_specs, out_specs=out_specs, check_vma=False
    )
```

profile of v0, /device:TPU:6, one launch (start us, length us, event | category | flops | bytes accessed | tf_op | source)
XLA Modules:
  0.0 771.0 jit_solution(8821121066339142544)
XLA Ops:
  47.4 123.4 %while.22 = (s32[]{:T(128)}, f32[8,1024]{1,0:T(8,128)S(1)}, f32[8]{0:T(128)}, f32[8,1024]{1,0:T(8,128)S(1)}, s32[]{:T(128)}, /*index=5*/s32[]{:T(128)}) while((s32[]{:T(128)}, f32[8,1024]{1,0:T(8,128)S(1)}, f32[8]{0:T(128)}, f32[8,1024]{1,0:T(8,128)S(1)}, s32[]{:T(128)}, /*index=5*/s32[]{:T(128)}) %tuple.59), condition=%wide.region_6.7_spmd.clone, body=%wide.region_5.6_spmd.clone.sunk | while | flops 40963 | bytes 196759 | solution.py:125
  62.1 6.3 collective-permute-start
  70.5 6.3 collective-permute-start
  78.9 6.3 collective-permute-start
  87.3 6.3 collective-permute-start
  95.7 6.3 collective-permute-start
  104.2 6.3 collective-permute-start
  112.6 6.3 collective-permute-start
  121.0 6.3 collective-permute-start
  129.4 6.3 collective-permute-start
  137.8 6.3 collective-permute-start
  146.2 6.3 collective-permute-start
  154.7 6.3 collective-permute-start
  163.1 6.3 collective-permute-start
  189.0 35.8 %all-gather.11.cloned.1.call-done = bf16[4,128,4096]{2,0,1:T(4,128)(2,1)} async-done(((bf16[4,128,512]{2,0,1:T(4,128)(2,1)}), bf16[4,128,4096]{2,0,1:T(4,128)(2,1)}) %all-gather.11.cloned.1.call-update) | async-done | bytes 4194320 | tf_op jit(solution)/shard_map/all_gather | solution.py:150
  229.3 34.2 %all-gather.9.cloned.1.call-done = bf16[4,128,4096]{2,0,1:T(4,128)(2,1)} async-done(((bf16[4,128,512]{2,0,1:T(4,128)(2,1)}), bf16[4,128,4096]{2,0,1:T(4,128)(2,1)}) %all-gather.9.cloned.1.call-update) | async-done | bytes 4194320 | tf_op jit(solution)/shard_map/all_gather | solution.py:151
  268.7 69.0 %all-gather.15.cloned.1.call-done = bf16[1,2048,2048]{2,1,0:T(8,128)(2,1)} async-done(((bf16[1,128,2048]{2,1,0:T(8,128)(2,1)}), bf16[1,2048,2048]{2,1,0:T(8,128)(2,1)}) %all-gather.15.cloned.1.call-update) | async-done | bytes 8388624 | tf_op jit(solution)/shard_map/all_gather | solution.py:156
  337.7 12.5 %fusion.56 = bf16[8,128,2048]{2,0,1:T(8,128)(2,1)S(1)} fusion(bf16[16,128,2048]{2,1,0:T(8,128)(2,1)} %bitcast.153, s32[16]{0:T(128)S(1)} %add_reduce_fusion, pred[16]{0:T(512)(128)(4,1)S(1)} %compare_reduce_fusion), kind=kOutput, calls=%fused_computation.58 | convolution fusion | flops 69206272 | bytes 12582992 | tf_op jit(solution)/shard_map/js,srf->jrf/dot_general | solution.py:42
  359.5 51.2 %all-gather.13.cloned.1.call-done = bf16[1,2048,2048]{2,1,0:T(8,128)(2,1)} async-done(((bf16[1,128,2048]{2,1,0:T(8,128)(2,1)}), bf16[1,2048,2048]{2,1,0:T(8,128)(2,1)}) %all-gather.13.cloned.1.call-update) | async-done | bytes 8388624 | tf_op jit(solution)/shard_map/all_gather | solution.py:157
  410.7 12.5 %fusion.53 = bf16[8,128,2048]{2,0,1:T(8,128)(2,1)S(1)} fusion(bf16[16,128,2048]{2,1,0:T(8,128)(2,1)} %bitcast.154, s32[16]{0:T(128)S(1)} %add_reduce_fusion, pred[16]{0:T(512)(128)(4,1)S(1)} %compare_reduce_fusion), kind=kOutput, calls=%fused_computation.57 | convolution fusion | flops 69206272 | bytes 12582992 | tf_op jit(solution)/shard_map/js,srf->jrf/dot_general | solution.py:42
  432.3 28.9 %all-reduce.3.cloned.1.call-done = (bf16[1024,768]{1,0:T(8,128)(2,1)}, bf16[1024,768]{1,0:T(8,128)(2,1)}) async-done(((bf16[1024,768]{1,0:T(8,128)(2,1)}, bf16[1024,768]{1,0:T(8,128)(2,1)}), (bf16[1024,768]{1,0:T(8,128)(2,1)}, bf16[1024,768]{1,0:T(8,128)(2,1)})) %all-reduce.3.cloned.1.call-update) | async-done | bytes 3145744 | tf_op jit(solution)/shard_map/psum | solution.py:168
  461.1 6.9 convolution_convert_fusion.1
  468.0 6.9 convolution_convert_fusion
  474.9 11.3 %copy.146 = bf16[16,128,2048]{2,1,0:T(8,128)(2,1)} copy(bf16[16,128,2048]{2,0,1:T(8,128)(2,1)} %convolution_convert_fusion) | data formatting | bytes 16777216 | tf_op jit(solution)/shard_map/convert_element_type | solution.py:187
  486.3 87.0 %reduce-scatter.2.cloned.1.call-done = bf16[128,2048]{1,0:T(8,128)(2,1)} async-done(((bf16[2048,2048]{1,0:T(8,128)(2,1)}), bf16[128,2048]{1,0:T(8,128)(2,1)}) %reduce-scatter.2.cloned.1.call-update) | async-done | bytes 524304 | tf_op jit(solution)/shard_map/reduce_scatter | solution.py:186
  573.4 7.8 %convolution_bitcast_fusion = f32[1,768,2048]{2,1,0:T(8,128)} fusion(bf16[1024,2048]{1,0:T(8,128)(2,1)} %bitcast.163, bf16[1024,768]{1,0:T(8,128)(2,1)S(1)} %copy-done.44), kind=kOutput, calls=%fused_computation.59 | convolution fusion | flops 3225944064 | bytes 12058624 | tf_op jit(solution)/shard_map/tf,td->fd/dot_general | solution.py:173
  581.3 6.1 convolution_bitcast_fusion.1
  587.4 19.6 %all-gather.17.cloned.1.call-done = bf16[1024,2048]{1,0:T(8,128)(2,1)} async-done(((bf16[128,2048]{1,0:T(8,128)(2,1)}), bf16[1024,2048]{1,0:T(8,128)(2,1)}) %all-gather.17.cloned.1.call-update) | async-done | bytes 4194320 | tf_op jit(solution)/shard_map/all_gather | solution.py:192
  636.8 117.3 %while.23 = (s32[]{:T(128)}, f32[8,1024]{1,0:T(8,128)S(1)}, f32[8]{0:T(128)S(1)}, f32[8,1024]{1,0:T(8,128)S(1)}, s32[]{:T(128)}, /*index=5*/s32[]{:T(128)}) while((s32[]{:T(128)}, f32[8,1024]{1,0:T(8,128)S(1)}, f32[8]{0:T(128)S(1)}, f32[8,1024]{1,0:T(8,128)S(1)}, s32[]{:T(128)}, /*index=5*/s32[]{:T(128)}) %tuple.80), condition=%wide.region_10.11_spmd.clone, body=%wide.region_9.10_spmd.clone.sunk | while | flops 40963 | bytes 196759 | solution.py:244
  646.6 5.8 collective-permute-done.1
  654.4 5.8 collective-permute-done.1
  724.7 5.9 collective-permute-done.1
  (288 shorter events, 266.0 us)
Async XLA Ops:
  7.2 217.5 %all-gather.11.cloned.1.call-start = ((), (), s32[]{:S(2)}) async-start(), calls=%async_computation.2 | async-start | bytes 4718592 | tf_op jit(solution)/shard_map/all_gather | solution.py:150
  62.1 7.7 %collective-permute-start = (bf16[8,1024]{1,0:T(8,128)(2,1)S(1)}, bf16[8,1024]{1,0:T(8,128)(2,1)S(1)}, u32[]{:S(2)}, u32[]{:S(2)}) collective-permute-start(bf16[8,1024]{1,0:T(8,128)(2,1)S(1)} %fusion.212), channel_id=1, source_target_pairs={{0,8},{8,16},{16,24},{24,32},{32,40},{40,48},{48,56},{56,64},{64,7... | collective-permute-start | bytes 49160 | tf_op jit(solution)/shard_map/while/body/eval_jaxpr/ppermute | solution.py:16
  70.5 7.7 %collective-permute-start = (bf16[8,1024]{1,0:T(8,128)(2,1)S(1)}, bf16[8,1024]{1,0:T(8,128)(2,1)S(1)}, u32[]{:S(2)}, u32[]{:S(2)}) collective-permute-start(bf16[8,1024]{1,0:T(8,128)(2,1)S(1)} %fusion.212), channel_id=1, source_target_pairs={{0,8},{8,16},{16,24},{24,32},{32,40},{40,48},{48,56},{56,64},{64,7... | collective-permute-start | bytes 49160 | tf_op jit(solution)/shard_map/while/body/eval_jaxpr/ppermute | solution.py:16
  78.9 7.7 %collective-permute-start = (bf16[8,1024]{1,0:T(8,128)(2,1)S(1)}, bf16[8,1024]{1,0:T(8,128)(2,1)S(1)}, u32[]{:S(2)}, u32[]{:S(2)}) collective-permute-start(bf16[8,1024]{1,0:T(8,128)(2,1)S(1)} %fusion.212), channel_id=1, source_target_pairs={{0,8},{8,16},{16,24},{24,32},{32,40},{40,48},{48,56},{56,64},{64,7... | collective-permute-start | bytes 49160 | tf_op jit(solution)/shard_map/while/body/eval_jaxpr/ppermute | solution.py:16
  87.3 7.7 %collective-permute-start = (bf16[8,1024]{1,0:T(8,128)(2,1)S(1)}, bf16[8,1024]{1,0:T(8,128)(2,1)S(1)}, u32[]{:S(2)}, u32[]{:S(2)}) collective-permute-start(bf16[8,1024]{1,0:T(8,128)(2,1)S(1)} %fusion.212), channel_id=1, source_target_pairs={{0,8},{8,16},{16,24},{24,32},{32,40},{40,48},{48,56},{56,64},{64,7... | collective-permute-start | bytes 49160 | tf_op jit(solution)/shard_map/while/body/eval_jaxpr/ppermute | solution.py:16
  95.7 7.7 %collective-permute-start = (bf16[8,1024]{1,0:T(8,128)(2,1)S(1)}, bf16[8,1024]{1,0:T(8,128)(2,1)S(1)}, u32[]{:S(2)}, u32[]{:S(2)}) collective-permute-start(bf16[8,1024]{1,0:T(8,128)(2,1)S(1)} %fusion.212), channel_id=1, source_target_pairs={{0,8},{8,16},{16,24},{24,32},{32,40},{40,48},{48,56},{56,64},{64,7... | collective-permute-start | bytes 49160 | tf_op jit(solution)/shard_map/while/body/eval_jaxpr/ppermute | solution.py:16
  104.2 7.7 %collective-permute-start = (bf16[8,1024]{1,0:T(8,128)(2,1)S(1)}, bf16[8,1024]{1,0:T(8,128)(2,1)S(1)}, u32[]{:S(2)}, u32[]{:S(2)}) collective-permute-start(bf16[8,1024]{1,0:T(8,128)(2,1)S(1)} %fusion.212), channel_id=1, source_target_pairs={{0,8},{8,16},{16,24},{24,32},{32,40},{40,48},{48,56},{56,64},{64,7... | collective-permute-start | bytes 49160 | tf_op jit(solution)/shard_map/while/body/eval_jaxpr/ppermute | solution.py:16
  112.6 7.7 %collective-permute-start = (bf16[8,1024]{1,0:T(8,128)(2,1)S(1)}, bf16[8,1024]{1,0:T(8,128)(2,1)S(1)}, u32[]{:S(2)}, u32[]{:S(2)}) collective-permute-start(bf16[8,1024]{1,0:T(8,128)(2,1)S(1)} %fusion.212), channel_id=1, source_target_pairs={{0,8},{8,16},{16,24},{24,32},{32,40},{40,48},{48,56},{56,64},{64,7... | collective-permute-start | bytes 49160 | tf_op jit(solution)/shard_map/while/body/eval_jaxpr/ppermute | solution.py:16
  121.0 7.7 %collective-permute-start = (bf16[8,1024]{1,0:T(8,128)(2,1)S(1)}, bf16[8,1024]{1,0:T(8,128)(2,1)S(1)}, u32[]{:S(2)}, u32[]{:S(2)}) collective-permute-start(bf16[8,1024]{1,0:T(8,128)(2,1)S(1)} %fusion.212), channel_id=1, source_target_pairs={{0,8},{8,16},{16,24},{24,32},{32,40},{40,48},{48,56},{56,64},{64,7... | collective-permute-start | bytes 49160 | tf_op jit(solution)/shard_map/while/body/eval_jaxpr/ppermute | solution.py:16
  129.4 7.7 %collective-permute-start = (bf16[8,1024]{1,0:T(8,128)(2,1)S(1)}, bf16[8,1024]{1,0:T(8,128)(2,1)S(1)}, u32[]{:S(2)}, u32[]{:S(2)}) collective-permute-start(bf16[8,1024]{1,0:T(8,128)(2,1)S(1)} %fusion.212), channel_id=1, source_target_pairs={{0,8},{8,16},{16,24},{24,32},{32,40},{40,48},{48,56},{56,64},{64,7... | collective-permute-start | bytes 49160 | tf_op jit(solution)/shard_map/while/body/eval_jaxpr/ppermute | solution.py:16
  137.8 7.7 %collective-permute-start = (bf16[8,1024]{1,0:T(8,128)(2,1)S(1)}, bf16[8,1024]{1,0:T(8,128)(2,1)S(1)}, u32[]{:S(2)}, u32[]{:S(2)}) collective-permute-start(bf16[8,1024]{1,0:T(8,128)(2,1)S(1)} %fusion.212), channel_id=1, source_target_pairs={{0,8},{8,16},{16,24},{24,32},{32,40},{40,48},{48,56},{56,64},{64,7... | collective-permute-start | bytes 49160 | tf_op jit(solution)/shard_map/while/body/eval_jaxpr/ppermute | solution.py:16
  146.2 7.7 %collective-permute-start = (bf16[8,1024]{1,0:T(8,128)(2,1)S(1)}, bf16[8,1024]{1,0:T(8,128)(2,1)S(1)}, u32[]{:S(2)}, u32[]{:S(2)}) collective-permute-start(bf16[8,1024]{1,0:T(8,128)(2,1)S(1)} %fusion.212), channel_id=1, source_target_pairs={{0,8},{8,16},{16,24},{24,32},{32,40},{40,48},{48,56},{56,64},{64,7... | collective-permute-start | bytes 49160 | tf_op jit(solution)/shard_map/while/body/eval_jaxpr/ppermute | solution.py:16
  154.7 7.7 %collective-permute-start = (bf16[8,1024]{1,0:T(8,128)(2,1)S(1)}, bf16[8,1024]{1,0:T(8,128)(2,1)S(1)}, u32[]{:S(2)}, u32[]{:S(2)}) collective-permute-start(bf16[8,1024]{1,0:T(8,128)(2,1)S(1)} %fusion.212), channel_id=1, source_target_pairs={{0,8},{8,16},{16,24},{24,32},{32,40},{40,48},{48,56},{56,64},{64,7... | collective-permute-start | bytes 49160 | tf_op jit(solution)/shard_map/while/body/eval_jaxpr/ppermute | solution.py:16
  163.1 7.7 %collective-permute-start = (bf16[8,1024]{1,0:T(8,128)(2,1)S(1)}, bf16[8,1024]{1,0:T(8,128)(2,1)S(1)}, u32[]{:S(2)}, u32[]{:S(2)}) collective-permute-start(bf16[8,1024]{1,0:T(8,128)(2,1)S(1)} %fusion.212), channel_id=1, source_target_pairs={{0,8},{8,16},{16,24},{24,32},{32,40},{40,48},{48,56},{56,64},{64,7... | collective-permute-start | bytes 49160 | tf_op jit(solution)/shard_map/while/body/eval_jaxpr/ppermute | solution.py:16
  186.1 77.5 %all-gather.9.cloned.1.call-start = ((), (), s32[]{:S(2)}) async-start(), calls=%async_computation.1 | async-start | bytes 4718592 | tf_op jit(solution)/shard_map/all_gather | solution.py:151
  188.9 148.8 %all-gather.15.cloned.1.call-start = ((), (), s32[]{:S(2)}) async-start(), calls=%async_computation.5 | async-start | bytes 8912896 | tf_op jit(solution)/shard_map/all_gather | solution.py:156
  229.3 181.4 %all-gather.13.cloned.1.call-start = ((), (), s32[]{:S(2)}) async-start(), calls=%async_computation.4 | async-start | bytes 8912896 | tf_op jit(solution)/shard_map/all_gather | solution.py:157
  268.1 193.0 %all-reduce.3.cloned.1.call-start = ((), (), s32[]{:S(2)}) async-start(), calls=%async_computation.7 | async-start | bytes 6291456 | tf_op jit(solution)/shard_map/psum | solution.py:168
  432.2 141.1 %reduce-scatter.2.cloned.1.call-start = ((), (), s32[]{:S(2)}) async-start(), calls=%async_computation.3 | async-start | bytes 8912896 | tf_op jit(solution)/shard_map/reduce_scatter | solution.py:186
  486.3 120.8 %all-gather.17.cloned.1.call-start = ((), (), s32[]{:S(2)}) async-start(), calls=%async_computation.6 | async-start | bytes 4718592 | tf_op jit(solution)/shard_map/all_gather | solution.py:192
  636.9 7.7 %collective-permute-start.1 = (bf16[8,1024]{1,0:T(8,128)(2,1)S(1)}, bf16[8,1024]{1,0:T(8,128)(2,1)S(1)}, u32[]{:S(2)}, u32[]{:S(2)}) collective-permute-start(bf16[8,1024]{1,0:T(8,128)(2,1)S(1)} %fusion.213), channel_id=1, source_target_pairs={{8,0},{16,8},{24,16},{32,24},{40,32},{48,40},{56,48},{64,56},{72,6... | collective-permute-start | bytes 49160 | tf_op jit(solution)/shard_map/while/body/eval_jaxpr/ppermute | solution.py:16
  644.7 7.7 %collective-permute-start.1 = (bf16[8,1024]{1,0:T(8,128)(2,1)S(1)}, bf16[8,1024]{1,0:T(8,128)(2,1)S(1)}, u32[]{:S(2)}, u32[]{:S(2)}) collective-permute-start(bf16[8,1024]{1,0:T(8,128)(2,1)S(1)} %fusion.213), channel_id=1, source_target_pairs={{8,0},{16,8},{24,16},{32,24},{40,32},{48,40},{56,48},{64,56},{72,6... | collective-permute-start | bytes 49160 | tf_op jit(solution)/shard_map/while/body/eval_jaxpr/ppermute | solution.py:16
  652.5 7.7 %collective-permute-start.1 = (bf16[8,1024]{1,0:T(8,128)(2,1)S(1)}, bf16[8,1024]{1,0:T(8,128)(2,1)S(1)}, u32[]{:S(2)}, u32[]{:S(2)}) collective-permute-start(bf16[8,1024]{1,0:T(8,128)(2,1)S(1)} %fusion.213), channel_id=1, source_target_pairs={{8,0},{16,8},{24,16},{32,24},{40,32},{48,40},{56,48},{64,56},{72,6... | collective-permute-start | bytes 49160 | tf_op jit(solution)/shard_map/while/body/eval_jaxpr/ppermute | solution.py:16
  660.3 7.7 %collective-permute-start.1 = (bf16[8,1024]{1,0:T(8,128)(2,1)S(1)}, bf16[8,1024]{1,0:T(8,128)(2,1)S(1)}, u32[]{:S(2)}, u32[]{:S(2)}) collective-permute-start(bf16[8,1024]{1,0:T(8,128)(2,1)S(1)} %fusion.213), channel_id=1, source_target_pairs={{8,0},{16,8},{24,16},{32,24},{40,32},{48,40},{56,48},{64,56},{72,6... | collective-permute-start | bytes 49160 | tf_op jit(solution)/shard_map/while/body/eval_jaxpr/ppermute | solution.py:16
  668.1 7.7 %collective-permute-start.1 = (bf16[8,1024]{1,0:T(8,128)(2,1)S(1)}, bf16[8,1024]{1,0:T(8,128)(2,1)S(1)}, u32[]{:S(2)}, u32[]{:S(2)}) collective-permute-start(bf16[8,1024]{1,0:T(8,128)(2,1)S(1)} %fusion.213), channel_id=1, source_target_pairs={{8,0},{16,8},{24,16},{32,24},{40,32},{48,40},{56,48},{64,56},{72,6... | collective-permute-start | bytes 49160 | tf_op jit(solution)/shard_map/while/body/eval_jaxpr/ppermute | solution.py:16
  675.9 7.7 %collective-permute-start.1 = (bf16[8,1024]{1,0:T(8,128)(2,1)S(1)}, bf16[8,1024]{1,0:T(8,128)(2,1)S(1)}, u32[]{:S(2)}, u32[]{:S(2)}) collective-permute-start(bf16[8,1024]{1,0:T(8,128)(2,1)S(1)} %fusion.213), channel_id=1, source_target_pairs={{8,0},{16,8},{24,16},{32,24},{40,32},{48,40},{56,48},{64,56},{72,6... | collective-permute-start | bytes 49160 | tf_op jit(solution)/shard_map/while/body/eval_jaxpr/ppermute | solution.py:16
  683.7 7.7 %collective-permute-start.1 = (bf16[8,1024]{1,0:T(8,128)(2,1)S(1)}, bf16[8,1024]{1,0:T(8,128)(2,1)S(1)}, u32[]{:S(2)}, u32[]{:S(2)}) collective-permute-start(bf16[8,1024]{1,0:T(8,128)(2,1)S(1)} %fusion.213), channel_id=1, source_target_pairs={{8,0},{16,8},{24,16},{32,24},{40,32},{48,40},{56,48},{64,56},{72,6... | collective-permute-start | bytes 49160 | tf_op jit(solution)/shard_map/while/body/eval_jaxpr/ppermute | solution.py:16
  691.6 7.7 %collective-permute-start.1 = (bf16[8,1024]{1,0:T(8,128)(2,1)S(1)}, bf16[8,1024]{1,0:T(8,128)(2,1)S(1)}, u32[]{:S(2)}, u32[]{:S(2)}) collective-permute-start(bf16[8,1024]{1,0:T(8,128)(2,1)S(1)} %fusion.213), channel_id=1, source_target_pairs={{8,0},{16,8},{24,16},{32,24},{40,32},{48,40},{56,48},{64,56},{72,6... | collective-permute-start | bytes 49160 | tf_op jit(solution)/shard_map/while/body/eval_jaxpr/ppermute | solution.py:16
  699.4 7.7 %collective-permute-start.1 = (bf16[8,1024]{1,0:T(8,128)(2,1)S(1)}, bf16[8,1024]{1,0:T(8,128)(2,1)S(1)}, u32[]{:S(2)}, u32[]{:S(2)}) collective-permute-start(bf16[8,1024]{1,0:T(8,128)(2,1)S(1)} %fusion.213), channel_id=1, source_target_pairs={{8,0},{16,8},{24,16},{32,24},{40,32},{48,40},{56,48},{64,56},{72,6... | collective-permute-start | bytes 49160 | tf_op jit(solution)/shard_map/while/body/eval_jaxpr/ppermute | solution.py:16
  707.2 7.7 %collective-permute-start.1 = (bf16[8,1024]{1,0:T(8,128)(2,1)S(1)}, bf16[8,1024]{1,0:T(8,128)(2,1)S(1)}, u32[]{:S(2)}, u32[]{:S(2)}) collective-permute-start(bf16[8,1024]{1,0:T(8,128)(2,1)S(1)} %fusion.213), channel_id=1, source_target_pairs={{8,0},{16,8},{24,16},{32,24},{40,32},{48,40},{56,48},{64,56},{72,6... | collective-permute-start | bytes 49160 | tf_op jit(solution)/shard_map/while/body/eval_jaxpr/ppermute | solution.py:16
  715.0 7.7 %collective-permute-start.1 = (bf16[8,1024]{1,0:T(8,128)(2,1)S(1)}, bf16[8,1024]{1,0:T(8,128)(2,1)S(1)}, u32[]{:S(2)}, u32[]{:S(2)}) collective-permute-start(bf16[8,1024]{1,0:T(8,128)(2,1)S(1)} %fusion.213), channel_id=1, source_target_pairs={{8,0},{16,8},{24,16},{32,24},{40,32},{48,40},{56,48},{64,56},{72,6... | collective-permute-start | bytes 49160 | tf_op jit(solution)/shard_map/while/body/eval_jaxpr/ppermute | solution.py:16
  722.8 7.8 %collective-permute-start.1 = (bf16[8,1024]{1,0:T(8,128)(2,1)S(1)}, bf16[8,1024]{1,0:T(8,128)(2,1)S(1)}, u32[]{:S(2)}, u32[]{:S(2)}) collective-permute-start(bf16[8,1024]{1,0:T(8,128)(2,1)S(1)} %fusion.213), channel_id=1, source_target_pairs={{8,0},{16,8},{24,16},{32,24},{40,32},{48,40},{56,48},{64,56},{72,6... | collective-permute-start | bytes 49160 | tf_op jit(solution)/shard_map/while/body/eval_jaxpr/ppermute | solution.py:16
  (52 other events, 946.2 us)
Sparse Core Ops, SparseCore 0:
  186.2 38.4 all-gather.10
  227.0 36.5 all-gather.8
  266.2 71.4 all-gather.14
  340.3 70.3 all-gather.12
  432.3 28.7 all-reduce.2
  486.4 86.8 reduce-scatter.1
  575.0 31.9 all-gather.16
where the time goes:
time: 781 us; the launch traced here: 771 us
  waiting for transfers between devices  434 us (56%)
  starting transfers between devices  121 us (15%)
  matrix products  119 us (15%)
  local copies, waits for them, and re-layouts  54.2 us (7%)
  other arithmetic  26.6 us (3%)
  between operations  15.5 us (2%)
    ppermute x30, starting transfers between devices, from_behind(): lax.ppermute(value, axis, [(source, source + steps) for source in range(f...  120 us
    ppermute x30, waiting for transfers between devices, from_behind(): lax.ppermute(value, axis, [(source, source + steps) for source in range(f...  109 us
    reduce_scatter x1, waiting for transfers between devices, per_device(): lax.psum_scatter(spread_rows.reshape(BLOCK * lax.axis_size('seq'), half_w...  87 us
    all_gather x1, waiting for transfers between devices, per_device(): lax.all_gather(h_block, 'seq', axis=0, tiled=True)  69 us
    all_gather x1, waiting for transfers between devices, per_device(): lax.all_gather(g_block, 'seq', axis=0, tiled=True)  51.2 us
    all_gather x1, waiting for transfers between devices, per_device(): lax.all_gather(h_pick, ('expert', 'mp'), axis=2, tiled=True)  35.8 us
    all_gather x1, waiting for transfers between devices, per_device(): lax.all_gather(g_pick, ('expert', 'mp'), axis=2, tiled=True)  34.2 us
    psum x1, waiting for transfers between devices, per_device(): lax.psum(rounded(jnp.dot(x_rows, up_local, preferred_element_type=jnp.flo...  28.9 us
  transfers between devices with their start and end apart: 37, of which 37 were waited for; matrix products, arithmetic and copies ran while one was open for 6% of the time, Pallas kernels for 0%

commit v1 on v0

--- a/solution.py
+++ b/solution.py
@@ -8,6 +8,11 @@
 BLOCK = 128
 spike_position_step = 0.3
 highest = lax.Precision.HIGHEST
+
+
+def tiled_gather(value, axis, dim):
+    copies = jnp.concatenate([value] * lax.axis_size(axis), axis=dim)
+    return lax.all_to_all(copies, axis, dim, dim, tiled=True)
 
 
 def from_behind(value, axis, steps):
@@ -147,7 +152,7 @@
         preferred_element_type=jnp.float32,
     ).astype(jnp.bfloat16)
     h_full, g_full = (
-        lax.all_gather(h_pick, ("expert", "mp"), axis=2, tiled=True),
+        tiled_gather(h_pick, ("expert", "mp"), 2),
         lax.all_gather(g_pick, ("expert", "mp"), axis=2, tiled=True),
     )
     h_block = narrow(h_full, exp_index, mp_index, half_width)

time: 781 us -> 772 us (0.988)
  waiting for transfers between devices: 434 us -> 410 us
  local copies, waits for them, and re-layouts: 54.2 us -> 73.1 us
    all_to_all x0 -> x1, waiting for transfers between devices: none -> 49.7 us  [tiled_gather(): return lax.all_to_all(copies, axis, dim, dim, tiled=True)]
    all_gather x1 -> x0, waiting for transfers between devices: 35.8 us -> none  [per_device(): lax.all_gather(h_pick, ('expert', 'mp'), axis=2, tiled=True)]
    all_gather x1, waiting for transfers between devices: 34.2 us -> 0.02 us  [per_device(): lax.all_gather(g_pick, ('expert', 'mp'), axis=2, tiled=True)]
    concatenate x0 -> x2, local copies, waits for them, and re-layouts: none -> 10.6 us  [tiled_gather(): copies = jnp.concatenate([value] * lax.axis_size(axis), axis=dim)]
  transfers between devices with their start and end apart: 37 -> 37, of which waited for: 37 -> 36; matrix products, arithmetic and copies ran while one was open for 6% -> 16% of each run, Pallas kernels for 0% -> 0%
where the time goes in v1:
time: 772 us; the launch traced here: 765 us
  waiting for transfers between devices  410 us (53%)
  starting transfers between devices  126 us (16%)
  matrix products  113 us (15%)
  local copies, waits for them, and re-layouts  73.1 us (9%)
  other arithmetic  26.4 us (3%)
  between operations  15.7 us (2%)
    ppermute x30, starting transfers between devices, from_behind(): lax.ppermute(value, axis, [(source, source + steps) for source in range(f...  120 us
    ppermute x30, waiting for transfers between devices, from_behind(): lax.ppermute(value, axis, [(source, source + steps) for source in range(f...  109 us
    reduce_scatter x1, waiting for transfers between devices, per_device(): lax.psum_scatter(spread_rows.reshape(BLOCK * lax.axis_size('seq'), half_w...  87 us
    all_gather x1, waiting for transfers between devices, per_device(): lax.all_gather(h_block, 'seq', axis=0, tiled=True)  65.2 us
    all_gather x1, waiting for transfers between devices, per_device(): lax.all_gather(g_block, 'seq', axis=0, tiled=True)  51.1 us
    all_to_all x1, waiting for transfers between devices, tiled_gather(): return lax.all_to_all(copies, axis, dim, dim, tiled=True)  49.7 us
    psum x1, waiting for transfers between devices, per_device(): lax.psum(rounded(jnp.dot(x_rows, up_local, preferred_element_type=jnp.flo...  28.9 us
    dot_general x2, matrix products, compact(): jnp.einsum('js,srf->jrf', select, shaped, preferred_element_type=jnp.floa...  25 us
  transfers between devices with their start and end apart: 37, of which 36 were waited for; matrix products, arithmetic and copies ran while one was open for 16% of the time, Pallas kernels for 0%

profile of v1, /device:TPU:6, one launch (start us, length us, event | category | flops | bytes accessed | tf_op | source)
XLA Modules:
  0.0 764.5 jit_solution(15535578040482635477)
XLA Ops:
  39.2 123.7 %while.22 = (s32[]{:T(128)}, f32[8,1024]{1,0:T(8,128)S(1)}, f32[8]{0:T(128)}, f32[8,1024]{1,0:T(8,128)S(1)}, s32[]{:T(128)}, /*index=5*/s32[]{:T(128)}) while((s32[]{:T(128)}, f32[8,1024]{1,0:T(8,128)S(1)}, f32[8]{0:T(128)}, f32[8,1024]{1,0:T(8,128)S(1)}, s32[]{:T(128)}, /*index=5*/s32[]{:T(128)}) %tuple.60), condition=%wide.region_6.7_spmd.clone, body=%wide.region_5.6_spmd.clone.sunk | while | flops 40963 | bytes 196759 | solution.py:130
  53.9 6.3 collective-permute-start
  62.3 6.3 collective-permute-start
  70.7 6.3 collective-permute-start
  79.2 6.3 collective-permute-start
  87.6 6.3 collective-permute-start
  96.0 6.3 collective-permute-start
  104.5 6.3 collective-permute-start
  112.9 6.3 collective-permute-start
  121.3 6.3 collective-permute-start
  129.8 6.3 collective-permute-start
  138.2 6.3 collective-permute-start
  146.6 6.3 collective-permute-start
  155.0 6.3 collective-permute-start
  189.9 9.6 %copy.180 = bf16[4,128,4096]{1,0,2:T(4,128)(2,1)} copy(bf16[4,128,4096]{2,0,1:T(4,128)(2,1)} %constant_dynamic-update-slice_fusion) | data formatting | bytes 8388608 | tf_op jit(solution)/shard_map/concatenate | solution.py:14
  204.8 49.7 %all-to-all-done = bf16[4,128,4096]{1,0,2:T(4,128)(2,1)} async-done(((bf16[4,128,4096]{1,0,2:T(4,128)(2,1)}), bf16[4,128,4096]{1,0,2:T(4,128)(2,1)}, u32[]{:S(2)}, u32[]{:S(2)}) %all-to-all-start) | async-done | bytes 4194336 | tf_op jit(solution)/shard_map/all_to_all | solution.py:15
  266.6 65.2 %all-gather.12.cloned.1.call-done = bf16[1,2048,2048]{2,1,0:T(8,128)(2,1)} async-done(((bf16[1,128,2048]{2,1,0:T(8,128)(2,1)}), bf16[1,2048,2048]{2,1,0:T(8,128)(2,1)}) %all-gather.12.cloned.1.call-update) | async-done | bytes 8388624 | tf_op jit(solution)/shard_map/all_gather | solution.py:161
  331.8 12.5 %fusion.56 = bf16[8,128,2048]{2,0,1:T(8,128)(2,1)S(1)} fusion(bf16[16,128,2048]{2,1,0:T(8,128)(2,1)} %bitcast.155, s32[16]{0:T(128)S(1)} %add_reduce_fusion, pred[16]{0:T(512)(128)(4,1)S(1)} %compare_reduce_fusion), kind=kOutput, calls=%fused_computation.58 | convolution fusion | flops 69206272 | bytes 12582992 | tf_op jit(solution)/shard_map/js,srf->jrf/dot_general | solution.py:47
  353.3 51.1 %all-gather.10.cloned.1.call-done = bf16[1,2048,2048]{2,1,0:T(8,128)(2,1)} async-done(((bf16[1,128,2048]{2,1,0:T(8,128)(2,1)}), bf16[1,2048,2048]{2,1,0:T(8,128)(2,1)}) %all-gather.10.cloned.1.call-update) | async-done | bytes 8388624 | tf_op jit(solution)/shard_map/all_gather | solution.py:162
  404.4 12.5 %fusion.53 = bf16[8,128,2048]{2,0,1:T(8,128)(2,1)S(1)} fusion(bf16[16,128,2048]{2,1,0:T(8,128)(2,1)} %bitcast.156, s32[16]{0:T(128)S(1)} %add_reduce_fusion, pred[16]{0:T(512)(128)(4,1)S(1)} %compare_reduce_fusion), kind=kOutput, calls=%fused_computation.57 | convolution fusion | flops 69206272 | bytes 12582992 | tf_op jit(solution)/shard_map/js,srf->jrf/dot_general | solution.py:47
  426.2 28.9 %all-reduce.3.cloned.1.call-done = (bf16[1024,768]{1,0:T(8,128)(2,1)}, bf16[1024,768]{1,0:T(8,128)(2,1)}) async-done(((bf16[1024,768]{1,0:T(8,128)(2,1)}, bf16[1024,768]{1,0:T(8,128)(2,1)}), (bf16[1024,768]{1,0:T(8,128)(2,1)}, bf16[1024,768]{1,0:T(8,128)(2,1)})) %all-reduce.3.cloned.1.call-update) | async-done | bytes 3145744 | tf_op jit(solution)/shard_map/psum | solution.py:173
  455.0 6.9 convolution_convert_fusion.1
  462.0 6.9 convolution_convert_fusion
  468.9 11.3 %copy.185 = bf16[16,128,2048]{2,1,0:T(8,128)(2,1)} copy(bf16[16,128,2048]{2,0,1:T(8,128)(2,1)} %convolution_convert_fusion) | data formatting | bytes 16777216 | tf_op jit(solution)/shard_map/convert_element_type | solution.py:192
  480.2 87.0 %reduce-scatter.2.cloned.1.call-done = bf16[128,2048]{1,0:T(8,128)(2,1)} async-done(((bf16[2048,2048]{1,0:T(8,128)(2,1)}), bf16[128,2048]{1,0:T(8,128)(2,1)}) %reduce-scatter.2.cloned.1.call-update) | async-done | bytes 524304 | tf_op jit(solution)/shard_map/reduce_scatter | solution.py:191
  567.4 7.8 %convolution_bitcast_fusion = f32[1,768,2048]{2,1,0:T(8,128)} fusion(bf16[1024,2048]{1,0:T(8,128)(2,1)} %bitcast.165, bf16[1024,768]{1,0:T(8,128)(2,1)S(1)} %copy-done.51), kind=kOutput, calls=%fused_computation.59 | convolution fusion | flops 3225944064 | bytes 12058624 | tf_op jit(solution)/shard_map/tf,td->fd/dot_general | solution.py:178
  575.2 6.1 convolution_bitcast_fusion.1
  581.3 19.5 %all-gather.14.cloned.1.call-done = bf16[1024,2048]{1,0:T(8,128)(2,1)} async-done(((bf16[128,2048]{1,0:T(8,128)(2,1)}), bf16[1024,2048]{1,0:T(8,128)(2,1)}) %all-gather.14.cloned.1.call-update) | async-done | bytes 4194320 | tf_op jit(solution)/shard_map/all_gather | solution.py:197
  630.5 117.3 %while.23 = (s32[]{:T(128)}, f32[8,1024]{1,0:T(8,128)S(1)}, f32[8]{0:T(128)S(1)}, f32[8,1024]{1,0:T(8,128)S(1)}, s32[]{:T(128)}, /*index=5*/s32[]{:T(128)}) while((s32[]{:T(128)}, f32[8,1024]{1,0:T(8,128)S(1)}, f32[8]{0:T(128)S(1)}, f32[8,1024]{1,0:T(8,128)S(1)}, s32[]{:T(128)}, /*index=5*/s32[]{:T(128)}) %tuple.79), condition=%wide.region_10.11_spmd.clone, body=%wide.region_9.10_spmd.clone.sunk | while | flops 40963 | bytes 196759 | solution.py:249
  640.3 5.8 collective-permute-done.1
  648.2 5.8 collective-permute-done.1
  718.5 5.9 collective-permute-done.1
  (309 shorter events, 274.0 us)
Async XLA Ops:
  7.2 253.9 %all-gather.8.cloned.1.call-start = ((), (), s32[]{:S(2)}) async-start(), calls=%async_computation.2 | async-start | bytes 4718592 | tf_op jit(solution)/shard_map/all_gather | solution.py:156
  53.9 7.7 %collective-permute-start = (bf16[8,1024]{1,0:T(8,128)(2,1)S(1)}, bf16[8,1024]{1,0:T(8,128)(2,1)S(1)}, u32[]{:S(2)}, u32[]{:S(2)}) collective-permute-start(bf16[8,1024]{1,0:T(8,128)(2,1)S(1)} %fusion.212), channel_id=1, source_target_pairs={{0,8},{8,16},{16,24},{24,32},{32,40},{40,48},{48,56},{56,64},{64,7... | collective-permute-start | bytes 49160 | tf_op jit(solution)/shard_map/while/body/eval_jaxpr/ppermute | solution.py:21
  62.3 7.7 %collective-permute-start = (bf16[8,1024]{1,0:T(8,128)(2,1)S(1)}, bf16[8,1024]{1,0:T(8,128)(2,1)S(1)}, u32[]{:S(2)}, u32[]{:S(2)}) collective-permute-start(bf16[8,1024]{1,0:T(8,128)(2,1)S(1)} %fusion.212), channel_id=1, source_target_pairs={{0,8},{8,16},{16,24},{24,32},{32,40},{40,48},{48,56},{56,64},{64,7... | collective-permute-start | bytes 49160 | tf_op jit(solution)/shard_map/while/body/eval_jaxpr/ppermute | solution.py:21
  70.7 7.7 %collective-permute-start = (bf16[8,1024]{1,0:T(8,128)(2,1)S(1)}, bf16[8,1024]{1,0:T(8,128)(2,1)S(1)}, u32[]{:S(2)}, u32[]{:S(2)}) collective-permute-start(bf16[8,1024]{1,0:T(8,128)(2,1)S(1)} %fusion.212), channel_id=1, source_target_pairs={{0,8},{8,16},{16,24},{24,32},{32,40},{40,48},{48,56},{56,64},{64,7... | collective-permute-start | bytes 49160 | tf_op jit(solution)/shard_map/while/body/eval_jaxpr/ppermute | solution.py:21
  79.2 7.7 %collective-permute-start = (bf16[8,1024]{1,0:T(8,128)(2,1)S(1)}, bf16[8,1024]{1,0:T(8,128)(2,1)S(1)}, u32[]{:S(2)}, u32[]{:S(2)}) collective-permute-start(bf16[8,1024]{1,0:T(8,128)(2,1)S(1)} %fusion.212), channel_id=1, source_target_pairs={{0,8},{8,16},{16,24},{24,32},{32,40},{40,48},{48,56},{56,64},{64,7... | collective-permute-start | bytes 49160 | tf_op jit(solution)/shard_map/while/body/eval_jaxpr/ppermute | solution.py:21
  87.6 7.7 %collective-permute-start = (bf16[8,1024]{1,0:T(8,128)(2,1)S(1)}, bf16[8,1024]{1,0:T(8,128)(2,1)S(1)}, u32[]{:S(2)}, u32[]{:S(2)}) collective-permute-start(bf16[8,1024]{1,0:T(8,128)(2,1)S(1)} %fusion.212), channel_id=1, source_target_pairs={{0,8},{8,16},{16,24},{24,32},{32,40},{40,48},{48,56},{56,64},{64,7... | collective-permute-start | bytes 49160 | tf_op jit(solution)/shard_map/while/body/eval_jaxpr/ppermute | solution.py:21
  96.0 7.7 %collective-permute-start = (bf16[8,1024]{1,0:T(8,128)(2,1)S(1)}, bf16[8,1024]{1,0:T(8,128)(2,1)S(1)}, u32[]{:S(2)}, u32[]{:S(2)}) collective-permute-start(bf16[8,1024]{1,0:T(8,128)(2,1)S(1)} %fusion.212), channel_id=1, source_target_pairs={{0,8},{8,16},{16,24},{24,32},{32,40},{40,48},{48,56},{56,64},{64,7... | collective-permute-start | bytes 49160 | tf_op jit(solution)/shard_map/while/body/eval_jaxpr/ppermute | solution.py:21
  104.5 7.7 %collective-permute-start = (bf16[8,1024]{1,0:T(8,128)(2,1)S(1)}, bf16[8,1024]{1,0:T(8,128)(2,1)S(1)}, u32[]{:S(2)}, u32[]{:S(2)}) collective-permute-start(bf16[8,1024]{1,0:T(8,128)(2,1)S(1)} %fusion.212), channel_id=1, source_target_pairs={{0,8},{8,16},{16,24},{24,32},{32,40},{40,48},{48,56},{56,64},{64,7... | collective-permute-start | bytes 49160 | tf_op jit(solution)/shard_map/while/body/eval_jaxpr/ppermute | solution.py:21
  112.9 7.7 %collective-permute-start = (bf16[8,1024]{1,0:T(8,128)(2,1)S(1)}, bf16[8,1024]{1,0:T(8,128)(2,1)S(1)}, u32[]{:S(2)}, u32[]{:S(2)}) collective-permute-start(bf16[8,1024]{1,0:T(8,128)(2,1)S(1)} %fusion.212), channel_id=1, source_target_pairs={{0,8},{8,16},{16,24},{24,32},{32,40},{40,48},{48,56},{56,64},{64,7... | collective-permute-start | bytes 49160 | tf_op jit(solution)/shard_map/while/body/eval_jaxpr/ppermute | solution.py:21
  121.3 7.7 %collective-permute-start = (bf16[8,1024]{1,0:T(8,128)(2,1)S(1)}, bf16[8,1024]{1,0:T(8,128)(2,1)S(1)}, u32[]{:S(2)}, u32[]{:S(2)}) collective-permute-start(bf16[8,1024]{1,0:T(8,128)(2,1)S(1)} %fusion.212), channel_id=1, source_target_pairs={{0,8},{8,16},{16,24},{24,32},{32,40},{40,48},{48,56},{56,64},{64,7... | collective-permute-start | bytes 49160 | tf_op jit(solution)/shard_map/while/body/eval_jaxpr/ppermute | solution.py:21
  129.8 7.7 %collective-permute-start = (bf16[8,1024]{1,0:T(8,128)(2,1)S(1)}, bf16[8,1024]{1,0:T(8,128)(2,1)S(1)}, u32[]{:S(2)}, u32[]{:S(2)}) collective-permute-start(bf16[8,1024]{1,0:T(8,128)(2,1)S(1)} %fusion.212), channel_id=1, source_target_pairs={{0,8},{8,16},{16,24},{24,32},{32,40},{40,48},{48,56},{56,64},{64,7... | collective-permute-start | bytes 49160 | tf_op jit(solution)/shard_map/while/body/eval_jaxpr/ppermute | solution.py:21
  138.2 7.7 %collective-permute-start = (bf16[8,1024]{1,0:T(8,128)(2,1)S(1)}, bf16[8,1024]{1,0:T(8,128)(2,1)S(1)}, u32[]{:S(2)}, u32[]{:S(2)}) collective-permute-start(bf16[8,1024]{1,0:T(8,128)(2,1)S(1)} %fusion.212), channel_id=1, source_target_pairs={{0,8},{8,16},{16,24},{24,32},{32,40},{40,48},{48,56},{56,64},{64,7... | collective-permute-start | bytes 49160 | tf_op jit(solution)/shard_map/while/body/eval_jaxpr/ppermute | solution.py:21
  146.6 7.7 %collective-permute-start = (bf16[8,1024]{1,0:T(8,128)(2,1)S(1)}, bf16[8,1024]{1,0:T(8,128)(2,1)S(1)}, u32[]{:S(2)}, u32[]{:S(2)}) collective-permute-start(bf16[8,1024]{1,0:T(8,128)(2,1)S(1)} %fusion.212), channel_id=1, source_target_pairs={{0,8},{8,16},{16,24},{24,32},{32,40},{40,48},{48,56},{56,64},{64,7... | collective-permute-start | bytes 49160 | tf_op jit(solution)/shard_map/while/body/eval_jaxpr/ppermute | solution.py:21
  155.0 7.7 %collective-permute-start = (bf16[8,1024]{1,0:T(8,128)(2,1)S(1)}, bf16[8,1024]{1,0:T(8,128)(2,1)S(1)}, u32[]{:S(2)}, u32[]{:S(2)}) collective-permute-start(bf16[8,1024]{1,0:T(8,128)(2,1)S(1)} %fusion.212), channel_id=1, source_target_pairs={{0,8},{8,16},{16,24},{24,32},{32,40},{40,48},{48,56},{56,64},{64,7... | collective-permute-start | bytes 49160 | tf_op jit(solution)/shard_map/while/body/eval_jaxpr/ppermute | solution.py:21
  199.5 55.0 %all-to-all-start = ((bf16[4,128,4096]{1,0,2:T(4,128)(2,1)}), bf16[4,128,4096]{1,0,2:T(4,128)(2,1)}, u32[]{:S(2)}, u32[]{:S(2)}) async-start(bf16[4,128,4096]{1,0,2:T(4,128)(2,1)} %copy.180), calls=%async_computation | async-start | bytes 8388608 | tf_op jit(solution)/shard_map/all_to_all | solution.py:15
  204.7 127.1 %all-gather.12.cloned.1.call-start = ((), (), s32[]{:S(2)}) async-start(), calls=%async_computation.5 | async-start | bytes 8912896 | tf_op jit(solution)/shard_map/all_gather | solution.py:161
  261.1 143.3 %all-gather.10.cloned.1.call-start = ((), (), s32[]{:S(2)}) async-start(), calls=%async_computation.4 | async-start | bytes 8912896 | tf_op jit(solution)/shard_map/all_gather | solution.py:162
  265.8 189.3 %all-reduce.3.cloned.1.call-start = ((), (), s32[]{:S(2)}) async-start(), calls=%async_computation.7 | async-start | bytes 6291456 | tf_op jit(solution)/shard_map/psum | solution.py:173
  426.1 141.1 %reduce-scatter.2.cloned.1.call-start = ((), (), s32[]{:S(2)}) async-start(), calls=%async_computation.3 | async-start | bytes 8912896 | tf_op jit(solution)/shard_map/reduce_scatter | solution.py:191
  480.2 120.6 %all-gather.14.cloned.1.call-start = ((), (), s32[]{:S(2)}) async-start(), calls=%async_computation.6 | async-start | bytes 4718592 | tf_op jit(solution)/shard_map/all_gather | solution.py:197
  630.6 7.7 %collective-permute-start.1 = (bf16[8,1024]{1,0:T(8,128)(2,1)S(1)}, bf16[8,1024]{1,0:T(8,128)(2,1)S(1)}, u32[]{:S(2)}, u32[]{:S(2)}) collective-permute-start(bf16[8,1024]{1,0:T(8,128)(2,1)S(1)} %fusion.213), channel_id=1, source_target_pairs={{8,0},{16,8},{24,16},{32,24},{40,32},{48,40},{56,48},{64,56},{72,6... | collective-permute-start | bytes 49160 | tf_op jit(solution)/shard_map/while/body/eval_jaxpr/ppermute | solution.py:21
  638.4 7.7 %collective-permute-start.1 = (bf16[8,1024]{1,0:T(8,128)(2,1)S(1)}, bf16[8,1024]{1,0:T(8,128)(2,1)S(1)}, u32[]{:S(2)}, u32[]{:S(2)}) collective-permute-start(bf16[8,1024]{1,0:T(8,128)(2,1)S(1)} %fusion.213), channel_id=1, source_target_pairs={{8,0},{16,8},{24,16},{32,24},{40,32},{48,40},{56,48},{64,56},{72,6... | collective-permute-start | bytes 49160 | tf_op jit(solution)/shard_map/while/body/eval_jaxpr/ppermute | solution.py:21
  646.2 7.7 %collective-permute-start.1 = (bf16[8,1024]{1,0:T(8,128)(2,1)S(1)}, bf16[8,1024]{1,0:T(8,128)(2,1)S(1)}, u32[]{:S(2)}, u32[]{:S(2)}) collective-permute-start(bf16[8,1024]{1,0:T(8,128)(2,1)S(1)} %fusion.213), channel_id=1, source_target_pairs={{8,0},{16,8},{24,16},{32,24},{40,32},{48,40},{56,48},{64,56},{72,6... | collective-permute-start | bytes 49160 | tf_op jit(solution)/shard_map/while/body/eval_jaxpr/ppermute | solution.py:21
  654.1 7.7 %collective-permute-start.1 = (bf16[8,1024]{1,0:T(8,128)(2,1)S(1)}, bf16[8,1024]{1,0:T(8,128)(2,1)S(1)}, u32[]{:S(2)}, u32[]{:S(2)}) collective-permute-start(bf16[8,1024]{1,0:T(8,128)(2,1)S(1)} %fusion.213), channel_id=1, source_target_pairs={{8,0},{16,8},{24,16},{32,24},{40,32},{48,40},{56,48},{64,56},{72,6... | collective-permute-start | bytes 49160 | tf_op jit(solution)/shard_map/while/body/eval_jaxpr/ppermute | solution.py:21
  661.9 7.7 %collective-permute-start.1 = (bf16[8,1024]{1,0:T(8,128)(2,1)S(1)}, bf16[8,1024]{1,0:T(8,128)(2,1)S(1)}, u32[]{:S(2)}, u32[]{:S(2)}) collective-permute-start(bf16[8,1024]{1,0:T(8,128)(2,1)S(1)} %fusion.213), channel_id=1, source_target_pairs={{8,0},{16,8},{24,16},{32,24},{40,32},{48,40},{56,48},{64,56},{72,6... | collective-permute-start | bytes 49160 | tf_op jit(solution)/shard_map/while/body/eval_jaxpr/ppermute | solution.py:21
  669.7 7.7 %collective-permute-start.1 = (bf16[8,1024]{1,0:T(8,128)(2,1)S(1)}, bf16[8,1024]{1,0:T(8,128)(2,1)S(1)}, u32[]{:S(2)}, u32[]{:S(2)}) collective-permute-start(bf16[8,1024]{1,0:T(8,128)(2,1)S(1)} %fusion.213), channel_id=1, source_target_pairs={{8,0},{16,8},{24,16},{32,24},{40,32},{48,40},{56,48},{64,56},{72,6... | collective-permute-start | bytes 49160 | tf_op jit(solution)/shard_map/while/body/eval_jaxpr/ppermute | solution.py:21
  677.5 7.7 %collective-permute-start.1 = (bf16[8,1024]{1,0:T(8,128)(2,1)S(1)}, bf16[8,1024]{1,0:T(8,128)(2,1)S(1)}, u32[]{:S(2)}, u32[]{:S(2)}) collective-permute-start(bf16[8,1024]{1,0:T(8,128)(2,1)S(1)} %fusion.213), channel_id=1, source_target_pairs={{8,0},{16,8},{24,16},{32,24},{40,32},{48,40},{56,48},{64,56},{72,6... | collective-permute-start | bytes 49160 | tf_op jit(solution)/shard_map/while/body/eval_jaxpr/ppermute | solution.py:21
  685.3 7.7 %collective-permute-start.1 = (bf16[8,1024]{1,0:T(8,128)(2,1)S(1)}, bf16[8,1024]{1,0:T(8,128)(2,1)S(1)}, u32[]{:S(2)}, u32[]{:S(2)}) collective-permute-start(bf16[8,1024]{1,0:T(8,128)(2,1)S(1)} %fusion.213), channel_id=1, source_target_pairs={{8,0},{16,8},{24,16},{32,24},{40,32},{48,40},{56,48},{64,56},{72,6... | collective-permute-start | bytes 49160 | tf_op jit(solution)/shard_map/while/body/eval_jaxpr/ppermute | solution.py:21
  693.1 7.7 %collective-permute-start.1 = (bf16[8,1024]{1,0:T(8,128)(2,1)S(1)}, bf16[8,1024]{1,0:T(8,128)(2,1)S(1)}, u32[]{:S(2)}, u32[]{:S(2)}) collective-permute-start(bf16[8,1024]{1,0:T(8,128)(2,1)S(1)} %fusion.213), channel_id=1, source_target_pairs={{8,0},{16,8},{24,16},{32,24},{40,32},{48,40},{56,48},{64,56},{72,6... | collective-permute-start | bytes 49160 | tf_op jit(solution)/shard_map/while/body/eval_jaxpr/ppermute | solution.py:21
  700.9 7.7 %collective-permute-start.1 = (bf16[8,1024]{1,0:T(8,128)(2,1)S(1)}, bf16[8,1024]{1,0:T(8,128)(2,1)S(1)}, u32[]{:S(2)}, u32[]{:S(2)}) collective-permute-start(bf16[8,1024]{1,0:T(8,128)(2,1)S(1)} %fusion.213), channel_id=1, source_target_pairs={{8,0},{16,8},{24,16},{32,24},{40,32},{48,40},{56,48},{64,56},{72,6... | collective-permute-start | bytes 49160 | tf_op jit(solution)/shard_map/while/body/eval_jaxpr/ppermute | solution.py:21
  708.7 7.7 %collective-permute-start.1 = (bf16[8,1024]{1,0:T(8,128)(2,1)S(1)}, bf16[8,1024]{1,0:T(8,128)(2,1)S(1)}, u32[]{:S(2)}, u32[]{:S(2)}) collective-permute-start(bf16[8,1024]{1,0:T(8,128)(2,1)S(1)} %fusion.213), channel_id=1, source_target_pairs={{8,0},{16,8},{24,16},{32,24},{40,32},{48,40},{56,48},{64,56},{72,6... | collective-permute-start | bytes 49160 | tf_op jit(solution)/shard_map/while/body/eval_jaxpr/ppermute | solution.py:21
  716.5 7.8 %collective-permute-start.1 = (bf16[8,1024]{1,0:T(8,128)(2,1)S(1)}, bf16[8,1024]{1,0:T(8,128)(2,1)S(1)}, u32[]{:S(2)}, u32[]{:S(2)}) collective-permute-start(bf16[8,1024]{1,0:T(8,128)(2,1)S(1)} %fusion.213), channel_id=1, source_target_pairs={{8,0},{16,8},{24,16},{32,24},{40,32},{48,40},{56,48},{64,56},{72,6... | collective-permute-start | bytes 49160 | tf_op jit(solution)/shard_map/while/body/eval_jaxpr/ppermute | solution.py:21
  (59 other events, 1035.0 us)
Sparse Core Ops, SparseCore 0:
  11.1 38.1 all-gather.7
  261.2 70.5 all-gather.11
  334.0 70.3 all-gather.9
  426.3 28.7 all-reduce.2
  480.3 86.8 reduce-scatter.1
  568.8 31.9 all-gather.13
